TPU v7x, 128 devices: a whole 4x4x4 slice. The times are simulated.
128 devices in a mesh: row: 8 (over x, core), col: 16 (over z, y).
Axes of the slice: x: 4, y: 4, z: 4, core: 2. Of those that a mesh axis runs over, the one named last changes fastest.
Arguments:
- left_factor: float32 [23, 8, 128, 16, 16, 128], P(None, 'row', None, None, 'col'), may hold values from -5 to 5
- pick_site: int32 [23, 8, 128], P(None, 'row'), may hold values from 0 to 131071
- noise: float32 [23, 8, 128], P(None, 'row'), may hold values from 2 to 5
Outputs:
- panels: float32 [8, 16, 184, 2, 128], P('row', 'col')
All inputs are finite; a program needn't handle non-finite values.
Results may differ from a plain program's by a relative error of at most 0.000064.
Values sent between devices are 32-bit elements; how exact they have to be, the bound alone decides.
No kernel may reach another device: no remote copies, remote signals or barrier semaphores. Data moves between devices by JAX's collectives and lax.ppermute only.
A program may use at most 128 MiB of HBM per device.

v0:
```python
import jax
import jax.numpy as jnp
from jax import lax
from jax.sharding import PartitionSpec as P

GRID_Y = 64
GRID_Z = 32
LATERAL = 24.0
VERTICAL = 6.0


def site_coords(site_ids):
    coord_x = site_ids // (GRID_Y * GRID_Z)
    coord_y = site_ids // GRID_Z % GRID_Y
    coord_z = site_ids % GRID_Z
    return jnp.stack([coord_x, coord_y, coord_z]).astype(jnp.float32)


def matern(row_coords, col_coords):
    lengths = (LATERAL, LATERAL, VERTICAL)
    squared = jnp.zeros((row_coords.shape[1], col_coords.shape[1]), jnp.float32)
    for dim_index in range(3):
        difference = (row_coords[dim_index][:, None] - col_coords[dim_index][None, :]) / lengths[
            dim_index
        ]
        squared = squared + difference * difference
    radius = jnp.sqrt(3.0 * squared)
    return (1.0 + radius) * jnp.exp(-radius)


def times_transposed(left_mat, right_mat):
    return lax.dot_general(
        left_mat,
        right_mat,
        (((1,), (1,)), ((), ())),
        precision=lax.Precision.HIGHEST,
        preferred_element_type=jnp.float32,
    )


def lower_inverse(square):
    factor = jnp.linalg.cholesky(square)
    return jax.scipy.linalg.solve_triangular(
        factor, jnp.eye(square.shape[0], dtype=jnp.float32), lower=True
    )


def body(left_factor, pick_site, noise):
    row_blocks, _, block_width, col_blocks, _, _ = left_factor.shape
    col_count = lax.axis_size("col")
    row_share = row_blocks * block_width // col_count
    row_index = lax.axis_index("row")
    col_index = lax.axis_index("col")
    local_rows = left_factor.reshape(row_blocks * block_width, col_blocks * block_width)
    site_flat = pick_site.reshape(row_blocks * block_width)
    noise_flat = noise.reshape(row_blocks * block_width)
    offset = col_index * row_share
    my_coords = site_coords(lax.dynamic_slice_in_dim(site_flat, offset, row_share))
    my_noise = lax.dynamic_slice_in_dim(noise_flat, offset, row_share)
    first_owner = (row_index == 0) & (col_index == 0)
    second_owner = (row_index == 1) & (col_index == 0)
    own_diag = jnp.diag(my_noise[:block_width])
    head_rows = local_rows[:block_width]
    head_info = jnp.concatenate(
        [site_coords(site_flat[:block_width]), noise_flat[None, :block_width]], axis=0
    )
    is_first = row_index == 0
    is_second = row_index == 1
    heads = jnp.concatenate(
        [jnp.where(is_first, head_rows, 0.0), jnp.where(is_second, head_rows, 0.0)], axis=0
    )
    info = jnp.concatenate(
        [jnp.where(is_first, head_info, 0.0), jnp.where(is_second, head_info, 0.0)], axis=1
    )
    heads, info = lax.psum((heads, info), "row")
    terms = lax.dot_general(
        local_rows.reshape(col_count, row_share, col_blocks * block_width),
        heads,
        (((2,), (1,)), ((), ())),
        precision=lax.Precision.HIGHEST,
        preferred_element_type=jnp.float32,
    )
    gram = lax.psum(times_transposed(heads, heads), "col")
    sums = lax.psum_scatter(terms, "col", scatter_dimension=0, tiled=False)
    first_coords = info[:3, :block_width]
    second_coords = info[:3, block_width:]
    first_diag = matern(first_coords, first_coords) - gram[:block_width, :block_width]
    first_diag = first_diag + jnp.diag(info[3, :block_width])
    first_inverse = lower_inverse(first_diag)
    cross_rows = times_transposed(
        matern(second_coords, first_coords) - gram[block_width:, :block_width], first_inverse
    )
    second_diag = (
        matern(second_coords, second_coords)
        - gram[block_width:, block_width:]
        - times_transposed(cross_rows, cross_rows)
    )
    second_diag = second_diag + jnp.diag(info[3, block_width:])
    second_inverse = lower_inverse(second_diag)
    first_cov = matern(my_coords, first_coords) - sums[:, :block_width]
    first_cov = first_cov.at[:block_width].add(jnp.where(first_owner, own_diag, 0.0))
    first_panel = times_transposed(first_cov, first_inverse)
    second_cov = (
        matern(my_coords, second_coords)
        - sums[:, block_width:]
        - times_transposed(first_panel, cross_rows)
    )
    second_cov = second_cov.at[:block_width].add(jnp.where(second_owner, own_diag, 0.0))
    second_panel = times_transposed(second_cov, second_inverse)
    stacked = jnp.stack([first_panel, second_panel], axis=1)
    return stacked.reshape(1, 1, row_share, 2, block_width)


def solution(mesh):
    placed = (P(None, "row", None, None, "col", None), P(None, "row", None), P(None, "row", None))
    return jax.shard_map(
        body,
        mesh=mesh,
        in_specs=placed,
        out_specs=P("row", "col", None, None, None),
        check_vma=False,
    )
```

profile of v0, /device:TPU:0, one launch (start us, length us, event | category | flops | bytes accessed | tf_op | source)
XLA Modules:
  0.0 291.8 jit_solution(3037362575774388247)
XLA Ops:
  6.5 6.9 %fusion.6 = (f32[128,16,128]{2,1,0:T(8,128)S(1)}, f32[128,16,128]{2,1,0:T(8,128)S(1)}) fusion(pred[]{:T(512)S(6)} %eq.34, f32[23,1,128,16,1,128]{5,4,3,2,1,0:T(1,128)} %param.10, pred[]{:T(512)S(6)} %eq.35), kind=kLoop, calls=%fused_computation.10 | loop fusion | flops 524288 | bytes 3145730 | tf_op jit(solution)/shard_map/jit(_where)/select_n | solution.py:70
  13.5 0.9 copy_bitcast_fusion
  14.3 1.5 pad_maximum_fusion
  15.9 0.5 broadcast.389
  16.4 66.7 %reduce.21 = f32[23,128,16,128]{3,2,1,0:T(8,128)} reduce(f32[23,1,128,16,1,128]{5,4,3,2,1,0:T(1,128)} %param.10, f32[]{:T(128)} %broadcast.389), dimensions={1,4}, to_apply=%param.10.reduce_sub_computation.3 | reduce | bytes 48234500 | tf_op args[0]
  83.1 26.4 %reshape_reshape.3 = f32[16,184,2048]{2,1,0:T(8,128)} reshape(f32[23,128,16,128]{3,2,1,0:T(8,128)} %reduce.21) | data formatting | bytes 48234496 | tf_op jit(solution)/shard_map/reshape;reshape | solution.py:77
  109.5 4.9 %fusion.60 = f32[256,256]{0,1:T(8,128)} fusion(f32[256,2048]{1,0:T(8,128)} %all-reduce.4.cloned.1.call-done), kind=kOutput, calls=%fused_computation.128 | convolution fusion | flops 1610612736 | bytes 2359296 | tf_op jit(solution)/shard_map/dot_general | solution.py:32
  114.5 0.2 reduce-scatter.4.cloned.1.call-start
  114.7 23.1 %fusion.2 = f32[16,184,256]{2,1,0:T(8,128)} fusion(f32[16,184,2048]{2,1,0:T(8,128)} %reshape_reshape.3, f32[256,2048]{1,0:T(8,128)S(1)} %copy-done), kind=kOutput, calls=%fused_computation.5 | convolution fusion | flops 18522046464 | bytes 29229056 | tf_op jit(solution)/shard_map/dot_general | solution.py:76
  137.8 0.7 copy-done.1
  138.8 14.7 %psum.21 = f32[4,256]{1,0:T(4,128)S(1)} all-reduce(f32[4,256]{1,0:T(4,128)S(1)} %pad_maximum_fusion.1), channel_id=1, replica_groups=mesh['row'=8,'col'=16] {'row'}, use_global_device_ids=true, to_apply=%region_0.1 | all-reduce | flops 1024 | bytes 8192 | tf_op jit(solution)/shard_map/psum | solution.py:75
  153.6 48.5 %all-reduce.6.cloned.1.call-done = f32[256,256]{0,1:T(8,128)} async-done(((f32[256,256]{0,1:T(8,128)}), f32[256,256]{0,1:T(8,128)}) %all-reduce.6.cloned.1.call-update) | async-done | bytes 262160 | tf_op jit(solution)/shard_map/psum | solution.py:83
  202.2 1.0 fusion.19
  203.3 1.0 fusion.23
  204.3 11.7 %cholesky.44 = f32[128,128]{1,0:T(8,128)S(1)} custom-call(f32[128,128]{1,0:T(8,128)S(1)} %fusion.23), custom_call_target="Cholesky" | custom-call | tf_op jit(solution)/shard_map/jit(cholesky)/cholesky | solution.py:42
  216.0 0.6 compare_reduce_fusion.1
  216.7 0.7 fusion.12
  217.3 9.8 %custom-call.6 = f32[1,128,128]{1,2,0:T(8,128)S(1)} custom-call(f32[1,128,128]{2,1,0:T(8,128)S(1)} %fusion.12), custom_call_target="InvertDiagBlocksLowerTriangular" | custom-call | tf_op jit(solution)/shard_map/jit(_solve_triangular)/triangular_solve | solution.py:43
  227.1 0.3 fusion.10
  227.4 1.2 fusion.18
  228.7 1.1 fusion.5
  229.9 11.7 %cholesky.55 = f32[128,128]{1,0:T(8,128)S(1)} custom-call(f32[128,128]{1,0:T(8,128)S(1)} %fusion.21), custom_call_target="Cholesky" | custom-call | tf_op jit(solution)/shard_map/jit(cholesky)/cholesky | solution.py:42
  241.7 0.6 compare_reduce_fusion
  242.3 0.7 fusion.13
  243.0 10.0 %custom-call.7 = f32[1,128,128]{1,2,0:T(8,128)S(1)} custom-call(f32[1,128,128]{2,1,0:T(8,128)S(1)} %fusion.13), custom_call_target="InvertDiagBlocksLowerTriangular" | custom-call | tf_op jit(solution)/shard_map/jit(_solve_triangular)/triangular_solve | solution.py:43
  253.0 0.3 fusion.8
  253.3 28.7 %reduce-scatter.4.cloned.1.call-done = f32[1,184,256]{2,1,0:T(8,128)} async-done(((f32[16,184,256]{2,1,0:T(8,128)}), f32[1,184,256]{2,1,0:T(8,128)}) %reduce-scatter.4.cloned.1.call-update) | async-done | bytes 188432
  281.9 1.1 copy.19
  283.2 0.4 fusion.61
  283.6 0.4 convolution_subtract_fusion
  284.0 0.4 convolution_bitcast_fusion
  284.5 0.8 copy.26
  (33 shorter events, 0.9 us)
Async XLA Ops:
  6.5 103.0 %all-reduce.4.cloned.1.call-start = ((), (), s32[]{:S(2)}) async-start(), calls=%async_computation.1 | async-start | bytes 4194304 | tf_op jit(solution)/shard_map/psum | solution.py:75
  15.8 186.3 %all-reduce.6.cloned.1.call-start = ((), (), s32[]{:S(2)}) async-start(), calls=%async_computation.2 | async-start | bytes 524288 | tf_op jit(solution)/shard_map/psum | solution.py:83
  109.5 5.2 %copy-start = (f32[256,2048]{1,0:T(8,128)S(1)}, f32[256,2048]{1,0:T(8,128)}, u32[]{:S(2)}) copy-start(f32[256,2048]{1,0:T(8,128)} %all-reduce.4.cloned.1.call-done) | copy-start | bytes 6291460
  114.5 167.5 %reduce-scatter.4.cloned.1.call-start = ((), (), s32[]{:S(2)}) async-start(), calls=%async_computation.3 | async-start | bytes 3203072
  137.8 0.7 copy-start.1
  137.8 0.7 copy-start.2
Sparse Core Ops, SparseCore 0:
  15.9 68.0 all-reduce.3
  114.6 87.5 all-reduce.5
  205.5 76.3 reduce-scatter.3
where the time goes:
time: 293 us; the launch traced here: 292 us
  other arithmetic  123 us (42%)
  waiting for transfers between devices  77.3 us (26%)
  matrix products  32.1 us (11%)
  local copies, waits for them, and re-layouts  30.6 us (10%)
  blocking collectives  14.7 us (5%)
  between operations  13.4 us (5%)
    unnamed x3, other arithmetic  66.7 us
    psum x1, waiting for transfers between devices, body(): gram = lax.psum(times_transposed(heads, heads), 'col')  48.5 us
    unnamed x4, waiting for transfers between devices  28.7 us
    another operation x1, local copies, waits for them, and re-layouts, body(): local_rows.reshape(col_count, row_share, col_blocks * block_width)  26.4 us
    another operation x6, other arithmetic, lower_inverse(): factor = jnp.linalg.cholesky(square)  24.8 us
    dot_general x1, matrix products, body(): lax.dot_general(local_rows.reshape(col_count, row_share, col_blocks * blo...  23.1 us
    another operation x4, other arithmetic, lower_inverse(): jax.scipy.linalg.solve_triangular(factor, jnp.eye(square.shape[0], dtype=...  21.1 us
    psum x1, blocking collectives, body(): heads, info = lax.psum((heads, info), 'row')  14.7 us
  transfers between devices with their start and end apart: 3, of which 2 were waited for; matrix products, arithmetic and copies ran while one was open for 58% of the time, Pallas kernels for 0%

commit v1 on v0

--- a/solution.py
+++ b/solution.py
@@ -2,11 +2,16 @@
 import jax.numpy as jnp
 from jax import lax
 from jax.sharding import PartitionSpec as P
+from jax.lax import all_gather
 
 GRID_Y = 64
 GRID_Z = 32
 LATERAL = 24.0
 VERTICAL = 6.0
+
+
+def node_fill(unit):
+    return jnp.sum(all_gather(unit, "col"), axis=0)
 
 
 def site_coords(site_ids):
@@ -80,7 +85,7 @@
         precision=lax.Precision.HIGHEST,
         preferred_element_type=jnp.float32,
     )
-    gram = lax.psum(times_transposed(heads, heads), "col")
+    gram = node_fill(times_transposed(heads, heads))
     sums = lax.psum_scatter(terms, "col", scatter_dimension=0, tiled=False)
     first_coords = info[:3, :block_width]
     second_coords = info[:3, block_width:]

time: 293 us -> 326 us (1.11)
  waiting for transfers between devices: 77.3 us -> 111 us
  matrix products: 32.1 us -> 28.7 us
    all_gather x0 -> x1, waiting for transfers between devices: none -> 51.6 us  [node_fill(): return jnp.sum(all_gather(unit, 'col'), axis=0)]
    psum x1 -> x0, waiting for transfers between devices: 48.5 us -> none  [body(): gram = lax.psum(times_transposed(heads, heads), 'col')]
    unnamed x4, waiting for transfers between devices: 28.7 us -> 59.4 us
    dot_general x6, matrix products: 8.48 us -> 4.42 us  [times_transposed(): lax.dot_general(left_mat, right_mat, (((1,), (1,)), ((), ())), precision=...]
  transfers between devices with their start and end apart: 3 -> 3, of which waited for: 2 -> 2; matrix products, arithmetic and copies ran while one was open for 58% -> 30% of each run, Pallas kernels for 0% -> 0%
where the time goes in v1:
time: 326 us; the launch traced here: 325 us
  other arithmetic  124 us (38%)
  waiting for transfers between devices  111 us (34%)
  local copies, waits for them, and re-layouts  31.7 us (10%)
  matrix products  28.7 us (9%)
  blocking collectives  15.3 us (5%)
  between operations  13.4 us (4%)
    unnamed x3, other arithmetic  66.8 us
    unnamed x4, waiting for transfers between devices  59.4 us
    all_gather x1, waiting for transfers between devices, node_fill(): return jnp.sum(all_gather(unit, 'col'), axis=0)  51.6 us
    another operation x1, local copies, waits for them, and re-layouts, body(): local_rows.reshape(col_count, row_share, col_blocks * block_width)  26.4 us
    another operation x6, other arithmetic, lower_inverse(): factor = jnp.linalg.cholesky(square)  25 us
    dot_general x1, matrix products, body(): lax.dot_general(local_rows.reshape(col_count, row_share, col_blocks * blo...  23.7 us
    another operation x4, other arithmetic, lower_inverse(): jax.scipy.linalg.solve_triangular(factor, jnp.eye(square.shape[0], dtype=...  20.9 us
    psum x1, blocking collectives, body(): heads, info = lax.psum((heads, info), 'row')  15.3 us
  transfers between devices with their start and end apart: 3, of which 2 were waited for; matrix products, arithmetic and copies ran while one was open for 30% of the time, Pallas kernels for 0%

profile of v1, /device:TPU:0, one launch (start us, length us, event | category | flops | bytes accessed | tf_op | source)
XLA Modules:
  0.0 324.6 jit_solution(7010772381882553838)
XLA Ops:
  6.5 6.9 %fusion.6 = (f32[128,16,128]{2,1,0:T(8,128)S(1)}, f32[128,16,128]{2,1,0:T(8,128)S(1)}) fusion(pred[]{:T(512)S(6)} %eq.34, f32[23,1,128,16,1,128]{5,4,3,2,1,0:T(1,128)} %param.10, pred[]{:T(512)S(6)} %eq.35), kind=kLoop, calls=%fused_computation.10 | loop fusion | flops 524288 | bytes 3145730 | tf_op jit(solution)/shard_map/jit(_where)/select_n | solution.py:75
  13.5 0.9 copy_bitcast_fusion
  14.3 1.5 pad_maximum_fusion
  15.8 0.2 reduce-scatter.4.cloned.1.call-start
  16.1 0.5 broadcast.389
  16.6 66.7 %reduce.21 = f32[23,128,16,128]{3,2,1,0:T(8,128)} reduce(f32[23,1,128,16,1,128]{5,4,3,2,1,0:T(1,128)} %param.10, f32[]{:T(128)} %broadcast.389), dimensions={1,4}, to_apply=%param.10.reduce_sub_computation.3 | reduce | bytes 48234500 | tf_op args[0]
  83.3 26.4 %reshape_reshape.3 = f32[16,184,2048]{2,1,0:T(8,128)} reshape(f32[23,128,16,128]{3,2,1,0:T(8,128)} %reduce.21) | data formatting | bytes 48234496 | tf_op jit(solution)/shard_map/reshape;reshape | solution.py:82
  109.7 23.7 %fusion.2 = f32[16,184,256]{2,1,0:T(8,128)} fusion(f32[16,184,2048]{2,1,0:T(8,128)} %reshape_reshape.3, f32[256,2048]{1,0:T(8,128)} %all-reduce.3.cloned.1.call-done), kind=kOutput, calls=%fused_computation.5 | convolution fusion | flops 18522046464 | bytes 29229056 | tf_op jit(solution)/shard_map/dot_general | solution.py:81
  133.5 1.5 copy-done
  135.0 2.6 fusion.61
  137.9 15.3 %psum.14 = f32[4,256]{1,0:T(4,128)S(1)} all-reduce(f32[4,256]{1,0:T(4,128)S(1)} %pad_maximum_fusion.1), channel_id=1, replica_groups=mesh['row'=8,'col'=16] {'row'}, use_global_device_ids=true, to_apply=%region_0.1 | all-reduce | flops 1024 | bytes 8192 | tf_op jit(solution)/shard_map/psum | solution.py:80
  153.3 59.3 %reduce-scatter.4.cloned.1.call-done = f32[1,184,256]{2,1,0:T(8,128)} async-done(((f32[16,184,256]{2,1,0:T(8,128)}), f32[1,184,256]{2,1,0:T(8,128)}) %reduce-scatter.4.cloned.1.call-update) | async-done | bytes 188432
  212.7 1.1 copy.20
  213.7 0.2 slice_subtract_fusion.1
  214.0 51.6 %all-gather.3.cloned.1.call-done = f32[4096,256]{1,0:T(8,128)} async-done(((f32[256,256]{1,0:T(8,128)}), f32[4096,256]{1,0:T(8,128)}) %all-gather.3.cloned.1.call-update) | async-done | bytes 4194320 | tf_op jit(solution)/shard_map/all_gather | solution.py:14
  265.5 2.5 reduce_sum.9
  268.5 11.7 %cholesky.44 = f32[128,128]{1,0:T(8,128)S(1)} custom-call(f32[128,128]{1,0:T(8,128)S(1)} %fusion.21), custom_call_target="Cholesky" | custom-call | tf_op jit(solution)/shard_map/jit(cholesky)/cholesky | solution.py:47
  280.3 0.6 compare_reduce_fusion.1
  280.9 0.7 fusion.12
  281.6 9.8 %custom-call.6 = f32[1,128,128]{1,2,0:T(8,128)S(1)} custom-call(f32[1,128,128]{2,1,0:T(8,128)S(1)} %fusion.12), custom_call_target="InvertDiagBlocksLowerTriangular" | custom-call | tf_op jit(solution)/shard_map/jit(_solve_triangular)/triangular_solve | solution.py:48
  291.4 0.3 fusion.10
  291.9 0.4 fusion.62
  292.3 0.4 fusion.22
  292.7 0.4 convolution_subtract_fusion
  293.1 0.3 fusion.5
  293.5 11.9 %cholesky.55 = f32[128,128]{1,0:T(8,128)S(1)} custom-call(f32[128,128]{1,0:T(8,128)S(1)} %fusion.19), custom_call_target="Cholesky" | custom-call | tf_op jit(solution)/shard_map/jit(cholesky)/cholesky | solution.py:47
  305.4 0.6 compare_reduce_fusion
  306.1 0.7 fusion.13
  306.7 9.8 %custom-call.7 = f32[1,128,128]{1,2,0:T(8,128)S(1)} custom-call(f32[1,128,128]{2,1,0:T(8,128)S(1)} %fusion.13), custom_call_target="InvertDiagBlocksLowerTriangular" | custom-call | tf_op jit(solution)/shard_map/jit(_solve_triangular)/triangular_solve | solution.py:48
  316.5 0.3 fusion.8
  316.9 0.4 convolution_bitcast_fusion
  317.3 0.8 copy.29
  (38 shorter events, 1.4 us)
Async XLA Ops:
  6.5 103.1 %all-reduce.3.cloned.1.call-start = ((), (), s32[]{:S(2)}) async-start(), calls=%async_computation.1 | async-start | bytes 4194304 | tf_op jit(solution)/shard_map/psum | solution.py:80
  15.8 196.8 %reduce-scatter.4.cloned.1.call-start = ((), (), s32[]{:S(2)}) async-start(), calls=%async_computation.3 | async-start | bytes 3203072
  133.4 1.6 copy-start
  133.4 4.2 %copy-start.1 = (s32[23,1,128]{2,1,0:T(1,128)S(1)}, s32[23,1,128]{2,1,0:T(1,128)}, u32[]{:S(2)}) copy-start(s32[23,1,128]{2,1,0:T(1,128)} %param.11) | copy-start | bytes 35332
  133.4 4.2 %copy-start.2 = (f32[23,1,128]{2,1,0:T(1,128)S(1)}, f32[23,1,128]{2,1,0:T(1,128)}, u32[]{:S(2)}) copy-start(f32[23,1,128]{2,1,0:T(1,128)} %param.12) | copy-start | bytes 35332
  133.5 132.1 %all-gather.3.cloned.1.call-start = ((), (), s32[]{:S(2)}) async-start(), calls=%async_computation.2 | async-start | bytes 4456448 | tf_op jit(solution)/shard_map/all_gather | solution.py:14
Sparse Core Ops, SparseCore 0:
  15.9 68.0 all-reduce.2
  133.6 79.0 reduce-scatter.3
  214.8 50.6 all-gather.2
